TPU v7x, 256 devices: a whole 4x4x8 slice. The times are simulated.
256 devices in a mesh: dp: 32 (over x, z_hi, core), expert: 8 (over z_lo, y).
Axes of the slice: x: 4, y: 4, z: 8 (z_hi: 4, z_lo: 2; z = z_hi * 2 + z_lo), core: 2. Of those that a mesh axis runs over, the one named last changes fastest.
Arguments:
- tokens: bfloat16 [65536, 2560], P(('dp', 'expert')), may hold values from -24 to 24
- routes: int32 [65536, 1], P(('dp', 'expert')), may hold values from 0 to 7; in each aligned block of 256 rows (0 to 255, 256 to 511, ...) at most 40 rows name the same one
- gate_levels: int32 [65536, 1], P(('dp', 'expert')), may hold values from 1 to 64
- w_gate: bfloat16 [8, 2560, 768], P('expert', 'dp'), may hold values from -0.125 to 0.125
- w_up: bfloat16 [8, 2560, 768], P('expert', 'dp'), may hold values from -0.125 to 0.125
- w_down: bfloat16 [8, 2560, 768], P('expert', 'dp'), may hold values from -0.21875 to 0.21875
- grad_out: bfloat16 [65536, 2560], P(('dp', 'expert')), may hold values from -24 to 24
Outputs:
- moe_out: bfloat16 [65536, 2560], P(('dp', 'expert'))
- grad_tokens: bfloat16 [65536, 2560], P(('dp', 'expert'))
- grad_gate: float32 [8, 2560, 768], P('expert', 'dp')
- grad_up: float32 [8, 2560, 768], P('expert', 'dp')
- grad_down: float32 [8, 2560, 768], P('expert', 'dp')
Inputs may be any that keep to these rules, and one draw needn't show every extreme that they name: `routes`: among the rows of one device, no expert is named by more than 40 tokens, a bound that some block reaches.
All inputs are finite; a program needn't handle non-finite values.
Results may differ from a plain program's by a relative error of at most 0.019.
Values may be sent and summed in bfloat16 or wider, within the bound.
No kernel may reach another device: no remote copies, remote signals or barrier semaphores. Data moves between devices by JAX's collectives and lax.ppermute only.
A program may use at most 128 MiB of HBM per device.

v0:
```python
import jax
import jax.numpy as jnp
from jax import lax
from jax.sharding import Mesh
from jax.sharding import PartitionSpec as P

TOP = 1
CHIPS = ("x", "zh")
DP = ("x", "zh", "core")


def contract_last(matrix_a, matrix_b):
    return lax.dot_general(
        matrix_a, matrix_b, (((1,), (1,)), ((), ())), preferred_element_type=jnp.float32
    )


def contract_first(matrix_a, matrix_b):
    return lax.dot_general(
        matrix_a, matrix_b, (((0,), (0,)), ((), ())), preferred_element_type=jnp.float32
    )


def swap_cores(value):
    return lax.ppermute(value, "core", perm=[(0, 1), (1, 0)])


def gather_weight(weight):
    own = lax.all_to_all(weight, "core", split_axis=1, concat_axis=0, tiled=True)
    own = lax.all_gather(own, CHIPS, axis=0, tiled=True)
    other = swap_cores(own)
    return jnp.concatenate([own, other], axis=1)


def scatter_grad(part):
    half = part.shape[1] // 2
    rounded = part.astype(jnp.bfloat16)
    arrived = swap_cores(rounded[:, half:])
    pair_sum = (rounded[:, :half].astype(jnp.float32) + arrived.astype(jnp.float32)).astype(
        jnp.bfloat16
    )
    chip_sum = lax.psum_scatter(pair_sum, CHIPS, scatter_dimension=0, tiled=True)
    block = lax.all_to_all(chip_sum, "core", split_axis=0, concat_axis=1, tiled=True)
    return block.astype(jnp.float32)


def shards(tokens, routes, gate_levels, w_gate, w_up, w_down, grad_out):
    experts = lax.axis_size("expert")
    tok_rows = tokens.shape[0]
    model_width = tokens.shape[1]
    capacity = min(tok_rows, tok_rows * TOP * 5 // (4 * experts))
    slot_count = experts * capacity
    expert_of = routes[:, 0]
    onehot = (expert_of[:, None] == jnp.arange(experts, dtype=jnp.int32)[None, :]).astype(jnp.int32)
    earlier = jnp.cumsum(onehot, axis=0) - onehot
    slot_rank = jnp.sum(earlier * onehot, axis=1)
    slot_index = expert_of * capacity + slot_rank
    source_row = (
        jnp.zeros((slot_count,), jnp.int32)
        .at[slot_index]
        .set(jnp.arange(tok_rows, dtype=jnp.int32))
    )
    filled = (
        jnp.zeros((slot_count, 1), jnp.bfloat16)
        .at[slot_index, 0]
        .set(jnp.ones((tok_rows,), jnp.bfloat16))
    )
    gate_weight = gate_levels.astype(jnp.float32) / 64.0

    def pack_rows(values):
        return (jnp.take(values, source_row, axis=0) * filled).reshape(
            experts, capacity, model_width
        )

    gate_full = gather_weight(w_gate[0])
    up_full = gather_weight(w_up[0])
    down_full = gather_weight(w_down[0])
    received = lax.all_to_all(
        pack_rows(tokens), "expert", split_axis=0, concat_axis=0, tiled=True
    ).reshape(slot_count, model_width)
    act_gate = jnp.dot(received, gate_full, preferred_element_type=jnp.float32)
    act_up = jnp.dot(received, up_full, preferred_element_type=jnp.float32)
    sigmoid_gate = jax.nn.sigmoid(act_gate)
    silu_gate = act_gate * sigmoid_gate
    hidden = (silu_gate * act_up).astype(jnp.bfloat16)
    expert_out = (
        contract_last(hidden, down_full)
        .astype(jnp.bfloat16)
        .reshape(experts, capacity, model_width)
    )
    returned = lax.all_to_all(
        expert_out, "expert", split_axis=0, concat_axis=0, tiled=True
    ).reshape(slot_count, model_width)
    moe_out = (gate_weight * jnp.take(returned, slot_index, axis=0).astype(jnp.float32)).astype(
        jnp.bfloat16
    )
    out_grad = (gate_weight * grad_out.astype(jnp.float32)).astype(jnp.bfloat16)
    grad_rows = lax.all_to_all(
        pack_rows(out_grad), "expert", split_axis=0, concat_axis=0, tiled=True
    ).reshape(slot_count, model_width)
    hidden_grad = jnp.dot(grad_rows, down_full, preferred_element_type=jnp.float32)
    gate_delta = (
        hidden_grad * act_up * sigmoid_gate * (1.0 + act_gate * (1.0 - sigmoid_gate))
    ).astype(jnp.bfloat16)
    up_delta = (hidden_grad * silu_gate).astype(jnp.bfloat16)
    token_grad = (contract_last(gate_delta, gate_full) + contract_last(up_delta, up_full)).astype(
        jnp.bfloat16
    )
    arrived = lax.all_to_all(
        token_grad.reshape(experts, capacity, model_width),
        "expert",
        split_axis=0,
        concat_axis=0,
        tiled=True,
    )
    grad_tokens = jnp.take(arrived.reshape(slot_count, model_width), slot_index, axis=0)
    grad_down = scatter_grad(contract_first(grad_rows, hidden))
    grad_gate = scatter_grad(contract_first(received, gate_delta))
    grad_up = scatter_grad(contract_first(received, up_delta))
    return (moe_out, grad_tokens, grad_gate[None], grad_up[None], grad_down[None])


def solution(mesh):
    dp_size, expert_size = mesh.devices.shape
    chips = dp_size // 2
    x_size = 4 if chips % 4 == 0 else 1
    grid = mesh.devices.reshape(x_size, chips // x_size, 2, expert_size)
    fine = Mesh(grid, DP + ("expert",))
    rows = P(DP + ("expert",), None)
    weights = P("expert", DP, None)
    in_specs = (rows, rows, rows, weights, weights, weights, rows)
    out_specs = (rows, rows, weights, weights, weights)
    return jax.shard_map(shards, mesh=fine, in_specs=in_specs, out_specs=out_specs, check_vma=False)
```

profile of v0, /device:TPU:1, one launch (start us, length us, event | category | flops | bytes accessed | tf_op | source)
XLA Modules:
  0.0 517.0 jit_solution(15889433307063467944)
XLA Ops:
  7.2 1.0 all_to_all.93
  8.3 7.4 %all_to_all.116 = bf16[80,2,384]{2,0,1:T(8,128)(2,1)} all-to-all(bf16[80,2,384]{2,0,1:T(8,128)(2,1)S(1)} %copy.26), channel_id=1, replica_groups=mesh['x'=4,'zh'=4,'core'=2,'expert'=8] {'core'}, dimensions={1} | all-to-all | bytes 245760 | tf_op jit(solution)/shard_map/all_to_all | solution.py:29
  15.8 0.9 all_to_all.89
  16.8 4.5 all_to_all.117
  21.4 0.9 all_to_all.85
  22.3 4.5 all_to_all.118
  26.9 0.6 reduce-window.6
  27.9 1.4 scatter_custom_fusion
  29.3 1.6 multiply_convert_fusion
  31.0 3.2 gather_fusion.2
  34.1 3.2 gather_fusion
  37.3 2.2 scatter_custom_fusion.1
  39.5 3.5 select_multiply_fusion
  43.0 4.3 all-to-all-start.5
  47.3 35.1 %all-gather.8.cloned.1.call-done = bf16[2560,384]{1,0:T(8,128)(2,1)} async-done(((bf16[160,384]{1,0:T(8,128)(2,1)}), bf16[2560,384]{1,0:T(8,128)(2,1)}) %all-gather.8.cloned.1.call-update) | async-done | bytes 1966096 | tf_op jit(solution)/shard_map/all_gather | solution.py:30
  82.4 0.5 collective-permute-start.2
  82.9 4.4 all-to-all-start
  87.4 53.1 %all-gather.6.cloned.1.call-done = bf16[2560,384]{1,0:T(8,128)(2,1)} async-done(((bf16[160,384]{1,0:T(8,128)(2,1)}), bf16[2560,384]{1,0:T(8,128)(2,1)}) %all-gather.6.cloned.1.call-update) | async-done | bytes 1966096 | tf_op jit(solution)/shard_map/all_gather | solution.py:30
  140.5 2.4 collective-permute-start.1
  142.9 56.5 %all-gather.4.cloned.1.call-done = bf16[2560,384]{1,0:T(8,128)(2,1)} async-done(((bf16[160,384]{1,0:T(8,128)(2,1)}), bf16[2560,384]{1,0:T(8,128)(2,1)}) %all-gather.4.cloned.1.call-update) | async-done | bytes 1966096 | tf_op jit(solution)/shard_map/all_gather | solution.py:30
  199.4 2.4 collective-permute-start
  202.0 1.7 constant_dynamic-update-slice_fusion.3
  203.7 0.6 copy-done.7
  204.2 1.6 constant_dynamic-update-slice_fusion.1
  205.8 1.9 constant_dynamic-update-slice_fusion.4
  207.8 4.6 constant_dynamic-update-slice_fusion.2
  212.4 2.9 fusion.10
  215.3 4.2 fusion.9
  219.5 1.9 constant_dynamic-update-slice_fusion
  221.4 4.4 multiply_convert_fusion.3
  225.9 4.0 convolution_convert_fusion.2
  230.1 1.4 collective-permute-start.3
  231.5 3.6 collective-permute-done.3
  235.1 1.9 add_convert_fusion.2
  237.1 3.7 convolution_convert_fusion.1
  241.0 0.7 collective-permute-start.4
  241.7 3.6 collective-permute-done.4
  245.2 1.9 add_convert_fusion.1
  247.1 4.8 convolution_convert_fusion.3
  251.9 4.7 all-to-all-start.4
  256.7 3.7 convolution_convert_fusion
  260.4 1.9 copy-done.4
  262.2 1.5 slice.48
  263.7 0.7 collective-permute-start.5
  264.4 3.9 fusion.11
  268.3 2.7 fusion
  271.0 15.7 %all-to-all-done.4 = bf16[8,40,2560]{2,1,0:T(8,128)(2,1)S(1)} async-done(((bf16[8,40,2560]{2,1,0:T(8,128)(2,1)}), bf16[8,40,2560]{2,1,0:T(8,128)(2,1)S(1)}, u32[]{:S(2)}, u32[]{:S(2)}) %all-to-all-start.4) | async-done | bytes 1638432 | tf_op jit(solution)/shard_map/all_to_all | solution.py:91
  286.7 3.9 all-to-all-start.6
  290.6 4.0 add_convert_fusion
  294.6 2.5 gather_fusion.1
  297.1 14.6 %all-to-all-done.6 = bf16[8,40,2560]{2,1,0:T(8,128)(2,1)S(1)} async-done(((bf16[8,40,2560]{2,1,0:T(8,128)(2,1)}), bf16[8,40,2560]{2,1,0:T(8,128)(2,1)S(1)}, u32[]{:S(2)}, u32[]{:S(2)}) %all-to-all-start.6) | async-done | bytes 1638432 | tf_op jit(solution)/shard_map/all_to_all | solution.py:109
  311.7 1.4 gather_fusion.3
  313.2 1.2 broadcast_select_fusion
  314.4 0.5 copy-done.3
  315.0 1.4 multiply_convert_fusion.1
  316.4 7.0 %reduce-scatter.4.cloned.1.call-done = bf16[160,384]{1,0:T(8,128)(2,1)} async-done(((bf16[2560,384]{1,0:T(8,128)(2,1)}), bf16[160,384]{1,0:T(8,128)(2,1)}) %reduce-scatter.4.cloned.1.call-update) | async-done | bytes 122896 | tf_op jit(solution)/shard_map/reduce_scatter | solution.py:42
  323.4 6.3 %all_to_all.119 = bf16[2,80,384]{2,1,0:T(8,128)(2,1)S(1)} all-to-all(bf16[2,80,384]{2,1,0:T(8,128)(2,1)} %bitcast.63), channel_id=1, replica_groups=mesh['x'=4,'zh'=4,'core'=2,'expert'=8] {'core'}, dimensions={0} | all-to-all | bytes 245760 | tf_op jit(solution)/shard_map/all_to_all | solution.py:43
  329.8 0.9 reshape.127
  330.7 82.8 %reduce-scatter.6.cloned.1.call-done = bf16[160,384]{1,0:T(8,128)(2,1)} async-done(((bf16[2560,384]{1,0:T(8,128)(2,1)}), bf16[160,384]{1,0:T(8,128)(2,1)}) %reduce-scatter.6.cloned.1.call-update) | async-done | bytes 122896 | tf_op jit(solution)/shard_map/reduce_scatter | solution.py:42
  413.5 6.6 %all_to_all.120 = bf16[2,80,384]{2,1,0:T(8,128)(2,1)S(1)} all-to-all(bf16[2,80,384]{2,1,0:T(8,128)(2,1)} %bitcast.64), channel_id=1, replica_groups=mesh['x'=4,'zh'=4,'core'=2,'expert'=8] {'core'}, dimensions={0} | all-to-all | bytes 245760 | tf_op jit(solution)/shard_map/all_to_all | solution.py:43
  420.2 0.9 reshape.128
  421.1 81.1 %reduce-scatter.8.cloned.1.call-done = bf16[160,384]{1,0:T(8,128)(2,1)} async-done(((bf16[2560,384]{1,0:T(8,128)(2,1)}), bf16[160,384]{1,0:T(8,128)(2,1)}) %reduce-scatter.8.cloned.1.call-update) | async-done | bytes 122896 | tf_op jit(solution)/shard_map/reduce_scatter | solution.py:42
  502.3 6.9 %all_to_all.121 = bf16[2,80,384]{2,1,0:T(8,128)(2,1)S(1)} all-to-all(bf16[2,80,384]{2,1,0:T(8,128)(2,1)} %bitcast.65), channel_id=1, replica_groups=mesh['x'=4,'zh'=4,'core'=2,'expert'=8] {'core'}, dimensions={0} | all-to-all | bytes 245760 | tf_op jit(solution)/shard_map/all_to_all | solution.py:43
  509.3 0.9 reshape.129
  (77 shorter events, 1.9 us)
Async XLA Ops:
  7.2 27.0 %copy-start = (bf16[256,2560]{1,0:T(8,128)(2,1)S(1)}, bf16[256,2560]{1,0:T(8,128)(2,1)}, u32[]{:S(2)}) copy-start(bf16[256,2560]{1,0:T(8,128)(2,1)} %param.11) | copy-start | bytes 3932164
  7.2 19.7 %copy-start.12 = (s32[256,1]{0,1:T(1,128)S(1)}, s32[256,1]{0,1:T(1,128)}, u32[]{:S(2)}) copy-start(s32[256,1]{0,1:T(1,128)} %param.12) | copy-start | bytes 3076
  7.2 22.1 %copy-start.13 = (s32[256,1]{0,1:T(1,128)S(1)}, s32[256,1]{0,1:T(1,128)}, u32[]{:S(2)}) copy-start(s32[256,1]{0,1:T(1,128)} %param.13) | copy-start | bytes 3076
  7.2 75.2 %all-gather.8.cloned.1.call-start = ((), (), s32[]{:S(2)}) async-start(), calls=%async_computation.15 | async-start | bytes 2088960 | tf_op jit(solution)/shard_map/all_gather | solution.py:30
  15.8 124.8 %all-gather.6.cloned.1.call-start = ((), (), s32[]{:S(2)}) async-start(), calls=%async_computation.14 | async-start | bytes 2088960 | tf_op jit(solution)/shard_map/all_gather | solution.py:30
  21.3 178.1 %all-gather.4.cloned.1.call-start = ((), (), s32[]{:S(2)}) async-start(), calls=%async_computation.13 | async-start | bytes 2088960 | tf_op jit(solution)/shard_map/all_gather | solution.py:30
  34.1 5.3 %copy-start.2 = (bf16[320,2560]{1,0:T(8,128)(2,1)S(1)}, bf16[320,2560]{1,0:T(8,128)(2,1)}, u32[]{:S(2)}) copy-start(bf16[320,2560]{1,0:T(8,128)(2,1)} %gather_fusion.2) | copy-start | bytes 4915204
  43.0 39.9 %all-to-all-start.5 = ((bf16[8,40,2560]{2,1,0:T(8,128)(2,1)}), bf16[8,40,2560]{2,1,0:T(8,128)(2,1)}, u32[]{:S(2)}, u32[]{:S(2)}) async-start(bf16[8,40,2560]{2,1,0:T(8,128)(2,1)} %bitcast.17), calls=%async_computation.5 | async-start | bytes 3276800 | tf_op jit(solution)/shard_map/all_to_all | solution.py:98
  82.4 119.3 %copy-start.5 = (bf16[2560,384]{1,0:T(8,128)(2,1)S(1)}, bf16[2560,384]{1,0:T(8,128)(2,1)}, u32[]{:S(2)}) copy-start(bf16[2560,384]{1,0:T(8,128)(2,1)} %all-gather.8.cloned.1.call-done) | copy-start | bytes 5898244
  82.4 123.4 %collective-permute-start.2 = (bf16[2560,384]{1,0:T(8,128)(2,1)}, bf16[2560,384]{1,0:T(8,128)(2,1)}, u32[]{:S(2)}, u32[]{:S(2)}) collective-permute-start(bf16[2560,384]{1,0:T(8,128)(2,1)} %all-gather.8.cloned.1.call-done), channel_id=1, source_target_pairs={{0,8},{8,0},{1,9},{9,1},{2,10},{10,2},{3,11},{11,3},{4,12},{12,4},... | collective-permute-start | bytes 5898248 | tf_op jit(solution)/shard_map/ppermute | solution.py:25
  82.9 132.3 %all-to-all-start = ((bf16[8,40,2560]{2,1,0:T(8,128)(2,1)}), bf16[8,40,2560]{2,1,0:T(8,128)(2,1)}, u32[]{:S(2)}, u32[]{:S(2)}) async-start(bf16[8,40,2560]{2,1,0:T(8,128)(2,1)} %bitcast.7), calls=%async_computation | async-start | bytes 3276800 | tf_op jit(solution)/shard_map/all_to_all | solution.py:78
  87.3 236.0 %reduce-scatter.4.cloned.1.call-start = ((), (), s32[]{:S(2)}) async-start(), calls=%async_computation.16 | async-start | bytes 2088960 | tf_op jit(solution)/shard_map/reduce_scatter | solution.py:42
  140.5 67.2 %collective-permute-start.1 = (bf16[2560,384]{1,0:T(8,128)(2,1)}, bf16[2560,384]{1,0:T(8,128)(2,1)}, u32[]{:S(2)}, u32[]{:S(2)}) collective-permute-start(bf16[2560,384]{1,0:T(8,128)(2,1)} %all-gather.6.cloned.1.call-done), channel_id=1, source_target_pairs={{0,8},{8,0},{1,9},{9,1},{2,10},{10,2},{3,11},{11,3},{4,12},{12,4},... | collective-permute-start | bytes 5898248 | tf_op jit(solution)/shard_map/ppermute | solution.py:25
  199.4 2.6 copy-start.6
  199.4 20.1 %collective-permute-start = (bf16[2560,384]{1,0:T(8,128)(2,1)}, bf16[2560,384]{1,0:T(8,128)(2,1)}, u32[]{:S(2)}, u32[]{:S(2)}) collective-permute-start(bf16[2560,384]{1,0:T(8,128)(2,1)} %all-gather.4.cloned.1.call-done), channel_id=1, source_target_pairs={{0,8},{8,0},{1,9},{9,1},{2,10},{10,2},{3,11},{11,3},{4,12},{12,4},... | collective-permute-start | bytes 5898248 | tf_op jit(solution)/shard_map/ppermute | solution.py:25
  202.0 2.3 copy-start.7
  207.7 4.6 copy-start.11
  215.2 4.2 copy-start.8
  221.4 4.4 copy-start.9
  225.8 4.1 copy-start.14
  225.8 21.3 %copy-start.16 = (bf16[320,768]{1,0:T(8,128)(2,1)}, bf16[320,768]{1,0:T(8,128)(2,1)S(1)}, u32[]{:S(2)}) copy-start(bf16[320,768]{1,0:T(8,128)(2,1)S(1)} %get-tuple-element.11) | copy-start | bytes 1474564
  230.1 5.0 collective-permute-start.3
  237.0 176.5 %reduce-scatter.6.cloned.1.call-start = ((), (), s32[]{:S(2)}) async-start(), calls=%async_computation.17 | async-start | bytes 2088960 | tf_op jit(solution)/shard_map/reduce_scatter | solution.py:42
  241.0 4.3 collective-permute-start.4
  251.9 4.7 copy-start.17
  251.9 34.7 %all-to-all-start.4 = ((bf16[8,40,2560]{2,1,0:T(8,128)(2,1)}), bf16[8,40,2560]{2,1,0:T(8,128)(2,1)S(1)}, u32[]{:S(2)}, u32[]{:S(2)}) async-start(bf16[8,40,2560]{2,1,0:T(8,128)(2,1)} %bitcast.15), calls=%async_computation.4 | async-start | bytes 3276800 | tf_op jit(solution)/shard_map/all_to_all | solution.py:91
  260.4 1.9 copy-start.4
  263.7 4.6 copy-start.10
  263.7 4.6 copy-start.15
  263.7 26.9 %collective-permute-start.5 = (bf16[2560,384]{1,0:T(8,128)(2,1)}, bf16[2560,384]{1,0:T(8,128)(2,1)}, u32[]{:S(2)}, u32[]{:S(2)}) collective-permute-start(bf16[2560,384]{1,0:T(8,128)(2,1)} %slice.48), channel_id=1, source_target_pairs={{0,8},{8,0},{1,9},{9,1},{2,10},{10,2},{3,11},{11,3},{4,12},{12,4},... | collective-permute-start | bytes 5898248 | tf_op jit(solution)/shard_map/ppermute | solution.py:25
  286.7 25.1 %all-to-all-start.6 = ((bf16[8,40,2560]{2,1,0:T(8,128)(2,1)}), bf16[8,40,2560]{2,1,0:T(8,128)(2,1)S(1)}, u32[]{:S(2)}, u32[]{:S(2)}) async-start(bf16[8,40,2560]{2,1,0:T(8,128)(2,1)} %bitcast.59), calls=%async_computation.6 | async-start | bytes 3276800 | tf_op jit(solution)/shard_map/all_to_all | solution.py:109
  290.6 211.7 %reduce-scatter.8.cloned.1.call-start = ((), (), s32[]{:S(2)}) async-start(), calls=%async_computation.18 | async-start | bytes 2088960 | tf_op jit(solution)/shard_map/reduce_scatter | solution.py:42
  313.2 1.8 copy-start.3
  329.6 180.5 %copy-start.1 = (bf16[256,2560]{1,0:T(8,128)(2,1)S(1)}, bf16[256,2560]{1,0:T(8,128)(2,1)}, u32[]{:S(2)}) copy-start(bf16[256,2560]{1,0:T(8,128)(2,1)} %param.11) | copy-start | bytes 3932164
Sparse Core Ops, SparseCore 0:
  15.9 66.5 all-gather.7
  84.9 55.5 all-gather.5
  143.0 56.3 all-gather.3
  237.2 86.1 reduce-scatter.3
  327.2 86.2 reduce-scatter.5
  416.9 85.3 reduce-scatter.7
where the time goes:
time: 518 us; the launch traced here: 517 us
  waiting for transfers between devices  353 us (68%)
  local copies, waits for them, and re-layouts  36.8 us (7%)
  blocking collectives  36.2 us (7%)
  matrix products  34.2 us (7%)
  starting transfers between devices  25.6 us (5%)
  other arithmetic  16.4 us (3%)
  between operations  14.6 us (3%)
    reduce_scatter x3, waiting for transfers between devices, scatter_grad(): lax.psum_scatter(pair_sum, CHIPS, scatter_dimension=0, tiled=True)  171 us
    all_gather x3, waiting for transfers between devices, gather_weight(): own = lax.all_gather(own, CHIPS, axis=0, tiled=True)  145 us
    all_to_all x3, blocking collectives, scatter_grad(): lax.all_to_all(chip_sum, 'core', split_axis=0, concat_axis=1, tiled=True)  19.7 us
    all_to_all x3, blocking collectives, gather_weight(): lax.all_to_all(weight, 'core', split_axis=1, concat_axis=0, tiled=True)  16.5 us
    all_to_all x1, waiting for transfers between devices, shards(): lax.all_to_all(expert_out, 'expert', split_axis=0, concat_axis=0, tiled=T...  15.7 us
    all_to_all x1, waiting for transfers between devices, shards(): lax.all_to_all(token_grad.reshape(experts, capacity, model_width), 'exper...  14.6 us
    dot_general x3, matrix products, contract_last(): lax.dot_general(matrix_a, matrix_b, (((1,), (1,)), ((), ())), preferred_e...  11.4 us
    dot_general x3, matrix products, contract_first(): lax.dot_general(matrix_a, matrix_b, (((0,), (0,)), ((), ())), preferred_e...  11.4 us
  transfers between devices with their start and end apart: 16, of which 10 were waited for; matrix products, arithmetic and copies ran while one was open for 13% of the time, Pallas kernels for 0%

commit v1 on v0

--- a/solution.py
+++ b/solution.py
@@ -27,7 +27,9 @@
 
 def gather_weight(weight):
     own = lax.all_to_all(weight, "core", split_axis=1, concat_axis=0, tiled=True)
-    own = lax.all_gather(own, CHIPS, axis=0, tiled=True)
+    own = jnp.concatenate(
+        lax.all_to_all(jnp.stack([own] * lax.axis_size(CHIPS)), CHIPS, 0, 0), axis=0
+    )
     other = swap_cores(own)
     return jnp.concatenate([own, other], axis=1)
 

time: 518 us -> 569 us (1.098)
  blocking collectives: 36.2 us -> 232 us
  waiting for transfers between devices: 353 us -> 217 us
  local copies, waits for them, and re-layouts: 36.8 us -> 28.3 us
    all_to_all x0 -> x4, blocking collectives: none -> 204 us  [the longest x3 179 us: gather_weight(): lax.all_to_all(jnp.stack([own] * lax.axis_size(CHIPS)), CHIPS, 0, 0)]
    all_gather x3 -> x0, waiting for transfers between devices: 145 us -> none  [gather_weight(): own = lax.all_gather(own, CHIPS, axis=0, tiled=True)]
    all_to_all x1, waiting for transfers between devices: 0.01 us -> 8.5 us  [shards(): lax.all_to_all(pack_rows(tokens), 'expert', split_axis=0, concat_axis=0,...]
    concatenate x3 -> x0, local copies, waits for them, and re-layouts: 8.47 us -> none  [gather_weight(): return jnp.concatenate([own, other], axis=1)]
    all_to_all x3 -> x2, blocking collectives: 16.5 us -> 8.3 us  [gather_weight(): lax.all_to_all(weight, 'core', split_axis=1, concat_axis=0, tiled=True)]
  transfers between devices with their start and end apart: 16 -> 13, of which waited for: 10 -> 9; matrix products, arithmetic and copies ran while one was open for 13% -> 11% of each run, Pallas kernels for 0% -> 0%
where the time goes in v1:
time: 569 us; the launch traced here: 567 us
  blocking collectives  232 us (41%)
  waiting for transfers between devices  217 us (38%)
  matrix products  33.6 us (6%)
  local copies, waits for them, and re-layouts  28.3 us (5%)
  starting transfers between devices  23.7 us (4%)
  other arithmetic  18.5 us (3%)
  between operations  14.1 us (2%)
    all_to_all x3, blocking collectives, gather_weight(): lax.all_to_all(jnp.stack([own] * lax.axis_size(CHIPS)), CHIPS, 0, 0)  179 us
    reduce_scatter x3, waiting for transfers between devices, scatter_grad(): lax.psum_scatter(pair_sum, CHIPS, scatter_dimension=0, tiled=True)  168 us
    all_to_all x1, blocking collectives, shards(): lax.all_to_all(pack_rows(out_grad), 'expert', split_axis=0, concat_axis=0...  25.1 us
    all_to_all x3, blocking collectives, scatter_grad(): lax.all_to_all(chip_sum, 'core', split_axis=0, concat_axis=1, tiled=True)  19.8 us
    all_to_all x1, waiting for transfers between devices, shards(): lax.all_to_all(expert_out, 'expert', split_axis=0, concat_axis=0, tiled=T...  14.3 us
    all_to_all x1, waiting for transfers between devices, shards(): lax.all_to_all(token_grad.reshape(experts, capacity, model_width), 'exper...  13.7 us
    ppermute x6, waiting for transfers between devices, swap_cores(): return lax.ppermute(value, 'core', perm=[(0, 1), (1, 0)])  12.3 us
    dot_general x3, matrix products, contract_last(): lax.dot_general(matrix_a, matrix_b, (((1,), (1,)), ((), ())), preferred_e...  11.6 us
  transfers between devices with their start and end apart: 13, of which 9 were waited for; matrix products, arithmetic and copies ran while one was open for 11% of the time, Pallas kernels for 0%

profile of v1, /device:TPU:1, one launch (start us, length us, event | category | flops | bytes accessed | tf_op | source)
XLA Modules:
  0.0 567.3 jit_solution(12946420057708611513)
XLA Ops:
  7.2 1.0 all_to_all.96
  8.2 0.7 copy.26
  8.9 6.6 %all-to-all-start.5 = ((bf16[80,2,384]{2,0,1:T(8,128)(2,1)}), bf16[80,2,384]{2,0,1:T(8,128)(2,1)S(1)}, u32[]{:S(2)}, u32[]{:S(2)}) async-start(bf16[80,2,384]{2,0,1:T(8,128)(2,1)} %copy.26), calls=%async_computation.5 | async-start | bytes 245760 | tf_op jit(solution)/shard_map/all_to_all | solution.py:29
  15.5 0.7 fusion.8
  16.2 0.6 reduce-window.6
  17.0 0.8 fusion.7
  17.8 0.7 compare_select_fusion
  18.5 1.4 scatter_custom_fusion
  19.9 0.7 convert_multiply_fusion
  20.6 1.6 multiply_convert_fusion
  22.2 3.2 gather_fusion.2
  25.4 3.2 gather_fusion
  28.6 0.7 copy.24
  29.3 2.2 scatter_custom_fusion.1
  31.5 3.1 select_multiply_fusion
  34.5 3.5 all_to_all.122
  38.0 4.8 all_to_all.123
  42.8 25.1 %all_to_all.124 = bf16[8,40,2560]{2,1,0:T(8,128)(2,1)} all-to-all(bf16[8,40,2560]{2,1,0:T(8,128)(2,1)S(1)} %bitcast.56), channel_id=1, replica_groups=mesh['x'=4,'zh'=4,'core'=2,'expert'=8] {'expert'}, dimensions={0} | all-to-all | bytes 3276800 | tf_op jit(solution)/shard_map/all_to_all | solution.py:100
  68.1 57.5 %all_to_all.125 = bf16[16,160,384]{2,1,0:T(8,128)(2,1)} all-to-all(bf16[16,160,384]{2,1,0:T(8,128)(2,1)S(1)} %stack.17), channel_id=1, replica_groups=mesh['x'=4,'zh'=4,'core'=2,'expert'=8] {'x','zh'}, dimensions={0} | all-to-all | bytes 3932160 | tf_op jit(solution)/shard_map/all_to_all | solution.py:31
  125.8 76.9 %all_to_all.126 = bf16[16,160,384]{2,1,0:T(8,128)(2,1)S(1)} all-to-all(bf16[16,160,384]{2,1,0:T(8,128)(2,1)S(1)} %stack.15), channel_id=1, replica_groups=mesh['x'=4,'zh'=4,'core'=2,'expert'=8] {'x','zh'}, dimensions={0} | all-to-all | bytes 3932160 | tf_op jit(solution)/shard_map/all_to_all | solution.py:31
  202.9 44.3 %all_to_all.127 = bf16[16,160,384]{2,1,0:T(8,128)(2,1)} all-to-all(bf16[16,160,384]{2,1,0:T(8,128)(2,1)S(1)} %stack.13), channel_id=1, replica_groups=mesh['x'=4,'zh'=4,'core'=2,'expert'=8] {'x','zh'}, dimensions={0} | all-to-all | bytes 3932160 | tf_op jit(solution)/shard_map/all_to_all | solution.py:31
  247.2 4.3 all-to-all-start
  251.5 2.2 collective-permute-start.2
  254.3 5.1 collective-permute-done.2
  259.4 1.3 copy-done.14
  260.7 3.5 fusion.1
  264.2 8.5 %all-to-all-done = bf16[8,40,2560]{2,1,0:T(8,128)(2,1)} async-done(((bf16[8,40,2560]{2,1,0:T(8,128)(2,1)}), bf16[8,40,2560]{2,1,0:T(8,128)(2,1)}, u32[]{:S(2)}, u32[]{:S(2)}) %all-to-all-start) | async-done | bytes 1638432 | tf_op jit(solution)/shard_map/all_to_all | solution.py:80
  272.7 3.6 fusion.3
  276.3 3.8 multiply_convert_fusion.3
  280.2 4.2 convolution_convert_fusion.2
  284.6 1.0 collective-permute-start.3
  285.5 3.6 collective-permute-done.3
  289.1 1.9 add_convert_fusion.2
  291.1 3.7 convolution_convert_fusion.1
  295.0 0.5 collective-permute-start.4
  295.4 3.6 collective-permute-done.4
  299.0 1.8 add_convert_fusion.1
  300.9 1.5 copy-done.9
  302.4 4.2 convolution_convert_fusion.3
  306.6 3.9 all-to-all-start.7
  310.6 3.3 convolution_convert_fusion
  313.9 1.8 copy-done.4
  315.7 1.5 slice.48
  318.1 3.0 fusion.2
  321.1 4.4 fusion
  325.5 14.3 %all-to-all-done.7 = bf16[8,40,2560]{2,1,0:T(8,128)(2,1)S(1)} async-done(((bf16[8,40,2560]{2,1,0:T(8,128)(2,1)}), bf16[8,40,2560]{2,1,0:T(8,128)(2,1)S(1)}, u32[]{:S(2)}, u32[]{:S(2)}) %all-to-all-start.7) | async-done | bytes 1638432 | tf_op jit(solution)/shard_map/all_to_all | solution.py:93
  339.8 4.2 all-to-all-start.9
  344.0 4.0 add_convert_fusion
  348.0 0.7 copy-done.13
  348.7 2.5 gather_fusion.1
  351.2 13.7 %all-to-all-done.9 = bf16[8,40,2560]{2,1,0:T(8,128)(2,1)S(1)} async-done(((bf16[8,40,2560]{2,1,0:T(8,128)(2,1)}), bf16[8,40,2560]{2,1,0:T(8,128)(2,1)S(1)}, u32[]{:S(2)}, u32[]{:S(2)}) %all-to-all-start.9) | async-done | bytes 1638432 | tf_op jit(solution)/shard_map/all_to_all | solution.py:111
  364.9 1.4 gather_fusion.3
  366.4 1.2 broadcast_select_fusion
  367.6 0.5 copy-done.3
  368.1 1.4 multiply_convert_fusion.1
  369.6 3.8 reduce-scatter.4.cloned.1.call-done
  373.4 6.6 %all_to_all.128 = bf16[2,80,384]{2,1,0:T(8,128)(2,1)S(1)} all-to-all(bf16[2,80,384]{2,1,0:T(8,128)(2,1)} %bitcast.73), channel_id=1, replica_groups=mesh['x'=4,'zh'=4,'core'=2,'expert'=8] {'core'}, dimensions={0} | all-to-all | bytes 245760 | tf_op jit(solution)/shard_map/all_to_all | solution.py:45
  380.1 0.9 reshape.148
  381.0 82.6 %reduce-scatter.6.cloned.1.call-done = bf16[160,384]{1,0:T(8,128)(2,1)} async-done(((bf16[2560,384]{1,0:T(8,128)(2,1)}), bf16[160,384]{1,0:T(8,128)(2,1)}) %reduce-scatter.6.cloned.1.call-update) | async-done | bytes 122896 | tf_op jit(solution)/shard_map/reduce_scatter | solution.py:44
  463.6 6.6 %all_to_all.129 = bf16[2,80,384]{2,1,0:T(8,128)(2,1)S(1)} all-to-all(bf16[2,80,384]{2,1,0:T(8,128)(2,1)} %bitcast.74), channel_id=1, replica_groups=mesh['x'=4,'zh'=4,'core'=2,'expert'=8] {'core'}, dimensions={0} | all-to-all | bytes 245760 | tf_op jit(solution)/shard_map/all_to_all | solution.py:45
  470.4 0.9 reshape.149
  471.3 81.9 %reduce-scatter.8.cloned.1.call-done = bf16[160,384]{1,0:T(8,128)(2,1)} async-done(((bf16[2560,384]{1,0:T(8,128)(2,1)}), bf16[160,384]{1,0:T(8,128)(2,1)}) %reduce-scatter.8.cloned.1.call-update) | async-done | bytes 122896 | tf_op jit(solution)/shard_map/reduce_scatter | solution.py:44
  553.1 6.6 %all_to_all.130 = bf16[2,80,384]{2,1,0:T(8,128)(2,1)S(1)} all-to-all(bf16[2,80,384]{2,1,0:T(8,128)(2,1)} %bitcast.75), channel_id=1, replica_groups=mesh['x'=4,'zh'=4,'core'=2,'expert'=8] {'core'}, dimensions={0} | all-to-all | bytes 245760 | tf_op jit(solution)/shard_map/all_to_all | solution.py:45
  559.9 0.9 reshape.150
  (72 shorter events, 3.3 us)
Async XLA Ops:
  7.2 18.2 %copy-start = (bf16[256,2560]{1,0:T(8,128)(2,1)S(1)}, bf16[256,2560]{1,0:T(8,128)(2,1)}, u32[]{:S(2)}) copy-start(bf16[256,2560]{1,0:T(8,128)(2,1)} %param.11) | copy-start | bytes 3932164
  8.9 25.6 %all-to-all-start.5 = ((bf16[80,2,384]{2,0,1:T(8,128)(2,1)}), bf16[80,2,384]{2,0,1:T(8,128)(2,1)S(1)}, u32[]{:S(2)}, u32[]{:S(2)}) async-start(bf16[80,2,384]{2,0,1:T(8,128)(2,1)} %copy.26), calls=%async_computation.5 | async-start | bytes 245760 | tf_op jit(solution)/shard_map/all_to_all | solution.py:29
  25.3 3.2 copy-start.11
  25.3 3.2 copy-start.12
  25.3 6.1 %copy-start.2 = (bf16[320,2560]{1,0:T(8,128)(2,1)S(1)}, bf16[320,2560]{1,0:T(8,128)(2,1)}, u32[]{:S(2)}) copy-start(bf16[320,2560]{1,0:T(8,128)(2,1)} %gather_fusion.2) | copy-start | bytes 4915204
  202.7 70.0 %copy-start.5 = (bf16[16,160,384]{2,1,0:T(8,128)(2,1)}, bf16[16,160,384]{2,1,0:T(8,128)(2,1)S(1)}, u32[]{:S(2)}) copy-start(bf16[16,160,384]{2,1,0:T(8,128)(2,1)S(1)} %all_to_all.126) | copy-start | bytes 5898244
  247.2 25.5 %all-to-all-start = ((bf16[8,40,2560]{2,1,0:T(8,128)(2,1)}), bf16[8,40,2560]{2,1,0:T(8,128)(2,1)}, u32[]{:S(2)}, u32[]{:S(2)}) async-start(bf16[8,40,2560]{2,1,0:T(8,128)(2,1)} %bitcast.7), calls=%async_computation | async-start | bytes 3276800 | tf_op jit(solution)/shard_map/all_to_all | solution.py:80
  251.5 121.9 %reduce-scatter.4.cloned.1.call-start = ((), (), s32[]{:S(2)}) async-start(), calls=%async_computation.16 | async-start | bytes 2088960 | tf_op jit(solution)/shard_map/reduce_scatter | solution.py:44
  251.5 7.9 %collective-permute-start.2 = (bf16[2560,384]{1,0:T(8,128)(2,1)}, bf16[2560,384]{1,0:T(8,128)(2,1)S(1)}, u32[]{:S(2)}, u32[]{:S(2)}) collective-permute-start(bf16[2560,384]{1,0:T(8,128)(2,1)} %bitcast.63), channel_id=1, source_target_pairs={{0,8},{8,0},{1,9},{9,1},{2,10},{10,2},{3,11},{11,3},{4,12},{12,4},... | collective-permute-start | bytes 5898248 | tf_op jit(solution)/shard_map/ppermute | solution.py:25
  253.8 18.9 %collective-permute-start.1 = (bf16[2560,384]{1,0:T(8,128)(2,1)S(1)}, bf16[2560,384]{1,0:T(8,128)(2,1)}, u32[]{:S(2)}, u32[]{:S(2)}) collective-permute-start(bf16[2560,384]{1,0:T(8,128)(2,1)S(1)} %bitcast.57), channel_id=1, source_target_pairs={{0,8},{8,0},{1,9},{9,1},{2,10},{10,2},{3,11},{11,3},{4,12},{12,4},... | collective-permute-start | bytes 5898248 | tf_op jit(solution)/shard_map/ppermute | solution.py:25
  253.9 22.4 %collective-permute-start = (bf16[2560,384]{1,0:T(8,128)(2,1)}, bf16[2560,384]{1,0:T(8,128)(2,1)}, u32[]{:S(2)}, u32[]{:S(2)}) collective-permute-start(bf16[2560,384]{1,0:T(8,128)(2,1)} %bitcast.60), channel_id=1, source_target_pairs={{0,8},{8,0},{1,9},{9,1},{2,10},{10,2},{3,11},{11,3},{4,12},{12,4},... | collective-permute-start | bytes 5898248 | tf_op jit(solution)/shard_map/ppermute | solution.py:25
  259.4 1.3 copy-start.14
  272.7 3.6 copy-start.7
  280.1 4.2 copy-start.15
  280.1 10.9 %copy-start.17 = (bf16[320,768]{1,0:T(8,128)(2,1)}, bf16[320,768]{1,0:T(8,128)(2,1)S(1)}, u32[]{:S(2)}) copy-start(bf16[320,768]{1,0:T(8,128)(2,1)S(1)} %get-tuple-element.10) | copy-start | bytes 1474564
  280.1 20.7 %copy-start.19 = (bf16[320,768]{1,0:T(8,128)(2,1)}, bf16[320,768]{1,0:T(8,128)(2,1)S(1)}, u32[]{:S(2)}) copy-start(bf16[320,768]{1,0:T(8,128)(2,1)S(1)} %get-tuple-element.11) | copy-start | bytes 1474564
  284.6 4.6 collective-permute-start.3
  291.0 172.6 %reduce-scatter.6.cloned.1.call-start = ((), (), s32[]{:S(2)}) async-start(), calls=%async_computation.17 | async-start | bytes 2088960 | tf_op jit(solution)/shard_map/reduce_scatter | solution.py:44
  295.0 4.1 collective-permute-start.4
  300.9 1.5 copy-start.9
  306.6 4.0 copy-start.10
  306.6 33.2 %all-to-all-start.7 = ((bf16[8,40,2560]{2,1,0:T(8,128)(2,1)}), bf16[8,40,2560]{2,1,0:T(8,128)(2,1)S(1)}, u32[]{:S(2)}, u32[]{:S(2)}) async-start(bf16[8,40,2560]{2,1,0:T(8,128)(2,1)} %bitcast.69), calls=%async_computation.7 | async-start | bytes 3276800 | tf_op jit(solution)/shard_map/all_to_all | solution.py:93
  313.9 1.9 copy-start.4
  315.7 2.3 copy-start.6
  315.7 2.3 copy-start.18
  317.2 3.9 copy-start.8
  317.2 3.9 copy-start.16
  317.2 26.8 %collective-permute-start.5 = (bf16[2560,384]{1,0:T(8,128)(2,1)}, bf16[2560,384]{1,0:T(8,128)(2,1)}, u32[]{:S(2)}, u32[]{:S(2)}) collective-permute-start(bf16[2560,384]{1,0:T(8,128)(2,1)} %slice.48), channel_id=1, source_target_pairs={{0,8},{8,0},{1,9},{9,1},{2,10},{10,2},{3,11},{11,3},{4,12},{12,4},... | collective-permute-start | bytes 5898248 | tf_op jit(solution)/shard_map/ppermute | solution.py:25
  339.8 25.1 %all-to-all-start.9 = ((bf16[8,40,2560]{2,1,0:T(8,128)(2,1)}), bf16[8,40,2560]{2,1,0:T(8,128)(2,1)S(1)}, u32[]{:S(2)}, u32[]{:S(2)}) async-start(bf16[8,40,2560]{2,1,0:T(8,128)(2,1)} %bitcast.68), calls=%async_computation.9 | async-start | bytes 3276800 | tf_op jit(solution)/shard_map/all_to_all | solution.py:111
  344.0 209.1 %reduce-scatter.8.cloned.1.call-start = ((), (), s32[]{:S(2)}) async-start(), calls=%async_computation.18 | async-start | bytes 2088960 | tf_op jit(solution)/shard_map/reduce_scatter | solution.py:44
  348.0 0.7 copy-start.13
  366.4 1.8 copy-start.3
  379.9 180.8 %copy-start.1 = (bf16[256,2560]{1,0:T(8,128)(2,1)S(1)}, bf16[256,2560]{1,0:T(8,128)(2,1)}, u32[]{:S(2)}) copy-start(bf16[256,2560]{1,0:T(8,128)(2,1)} %param.11) | copy-start | bytes 3932164
Sparse Core Ops, SparseCore 0:
  291.1 82.1 reduce-scatter.3
  377.3 86.2 reduce-scatter.5
  467.1 85.9 reduce-scatter.7
